TPU v7x, 128 devices: a whole 4x4x4 slice. The times are simulated.
128 devices in a mesh: rep: 64 (over z, y, x_hi, core), shard: 2 (over x_lo).
Axes of the slice: x: 4 (x_hi: 2, x_lo: 2; x = x_hi * 2 + x_lo), y: 4, z: 4, core: 2. Of those that a mesh axis runs over, the one named last changes fastest.
Arguments:
- grad_xproj: bfloat16 [256, 2, 3072, 128], P(('rep', 'shard')), may hold values from -32 to 32
- grad_chan: bfloat16 [256, 2, 118, 3072], P(('rep', 'shard')), may hold values from -32 to 32
- grad_embed: bfloat16 [256, 1024, 1536], P(('rep', 'shard')), may hold values from -32 to 32
- weight_xproj: float32 [2, 3072, 128], P(None, 'shard'), may hold values from -0.3125 to 0.3125
- weight_chan: float32 [2, 118, 3072], P(None, None, 'shard'), may hold values from -0.3125 to 0.3125
- weight_embed: float32 [1024, 1536], P('shard'), may hold values from -0.3125 to 0.3125
- moment_xproj: float32 [2, 3072, 128], P(None, 'shard'), may hold values from -0.015625 to 0.015625
- moment_chan: float32 [2, 118, 3072], P(None, None, 'shard'), may hold values from -0.015625 to 0.015625
- moment_embed: float32 [1024, 1536], P('shard'), may hold values from -0.015625 to 0.015625
- second_xproj: float32 [2, 3072, 128], P(None, 'shard'), may hold values from 1e-08 to 1e-05
- second_chan: float32 [2, 118, 3072], P(None, None, 'shard'), may hold values from 1e-08 to 1e-05
- second_embed: float32 [1024, 1536], P('shard'), may hold values from 1e-08 to 1e-05
Outputs:
- new_weight_xproj: float32 [2, 3072, 128], P(None, 'shard')
- new_weight_chan: float32 [2, 118, 3072], P(None, None, 'shard')
- new_weight_embed: float32 [1024, 1536], P('shard')
- new_moment_xproj: float32 [2, 3072, 128], P(None, 'shard')
- new_moment_chan: float32 [2, 118, 3072], P(None, None, 'shard')
- new_moment_embed: float32 [1024, 1536], P('shard')
- new_second_xproj: float32 [2, 3072, 128], P(None, 'shard')
- new_second_chan: float32 [2, 118, 3072], P(None, None, 'shard')
- new_second_embed: float32 [1024, 1536], P('shard')
- full_xproj: bfloat16 [2, 3072, 128], replicated
- full_chan: bfloat16 [2, 118, 3072], replicated
- full_embed: bfloat16 [1024, 1536], replicated
- pre_norm: float32 [1], replicated
All inputs are finite; a program needn't handle non-finite values.
Results may differ from a plain program's by a relative error of at most 0.00085.
Values may be sent and summed in bfloat16 or wider, within the bound.
No kernel may reach another device: no remote copies, remote signals or barrier semaphores. Data moves between devices by JAX's collectives and lax.ppermute only.
A program may use at most 448 MiB of HBM per device.

v0:
```python
import jax
import jax.numpy as jnp
from jax import lax
from jax.sharding import PartitionSpec as P

beta_one = 0.9
beta_two = 0.999
learn_rate = 0.003
decay_rate = 0.1
epsilon = 1e-08
correct_one = 0.9999734386011124
correct_two = 0.09520785288629094


def adamw_update(weight, moment, second, gradient, clip_factor):
    clipped = clip_factor * gradient
    new_moment = beta_one * moment + (1.0 - beta_one) * clipped
    new_second = beta_two * second + (1.0 - beta_two) * clipped * clipped
    step_size = new_moment / correct_one / (jnp.sqrt(new_second / correct_two) + epsilon)
    new_weight = weight - learn_rate * (step_size + decay_rate * weight)
    return (new_weight, new_moment, new_second)


def on_device(
    grad_xproj,
    grad_chan,
    grad_embed,
    weight_xproj,
    weight_chan,
    weight_embed,
    moment_xproj,
    moment_chan,
    moment_embed,
    second_xproj,
    second_chan,
    second_embed,
):
    count_rep = lax.axis_size("rep")
    count_shard = lax.axis_size("shard")
    summed_x = jnp.sum(grad_xproj, axis=0, dtype=jnp.float32)
    summed_c = jnp.sum(grad_chan, axis=0, dtype=jnp.float32)
    summed_e = jnp.sum(grad_embed, axis=0, dtype=jnp.float32)
    group = (
        lax.psum_scatter(
            summed_x.astype(jnp.bfloat16), "shard", scatter_dimension=1, tiled=True
        ).astype(jnp.float32),
        lax.psum_scatter(
            summed_c.astype(jnp.bfloat16), "shard", scatter_dimension=2, tiled=True
        ).astype(jnp.float32),
        lax.psum_scatter(
            summed_e.astype(jnp.bfloat16), "shard", scatter_dimension=0, tiled=True
        ).astype(jnp.float32),
    )
    blocks = lax.psum((group[0], group[1], group[2]), "rep")
    inverse = 1.0 / (grad_xproj.shape[0] * count_rep * count_shard)
    mean_x = blocks[0] * inverse
    mean_c = blocks[1] * inverse
    mean_e = blocks[2] * inverse
    partial_squares = jnp.sum(mean_x * mean_x) + jnp.sum(mean_c * mean_c) + jnp.sum(mean_e * mean_e)
    squares = lax.psum(partial_squares, "shard")
    norm_value = jnp.sqrt(squares)
    clip_factor = jnp.minimum(1.0, 1.0 / (norm_value + 1e-06))
    wx, mx, vx = adamw_update(weight_xproj, moment_xproj, second_xproj, mean_x, clip_factor)
    wc, mc, vc = adamw_update(weight_chan, moment_chan, second_chan, mean_c, clip_factor)
    we, me, ve = adamw_update(weight_embed, moment_embed, second_embed, mean_e, clip_factor)
    gathered = (
        lax.all_gather(wx.astype(jnp.bfloat16), "shard", axis=1, tiled=True),
        lax.all_gather(wc.astype(jnp.bfloat16), "shard", axis=2, tiled=True),
        lax.all_gather(we.astype(jnp.bfloat16), "shard", axis=0, tiled=True),
    )
    return (
        wx,
        wc,
        we,
        mx,
        mc,
        me,
        vx,
        vc,
        ve,
        gathered[0],
        gathered[1],
        gathered[2],
        jnp.reshape(norm_value, (1,)),
    )


def solution(mesh):
    placed = (
        P(("rep", "shard"), None, None, None),
        P(("rep", "shard"), None, None, None),
        P(("rep", "shard"), None, None),
        P(None, "shard", None),
        P(None, None, "shard"),
        P("shard", None),
        P(None, "shard", None),
        P(None, None, "shard"),
        P("shard", None),
        P(None, "shard", None),
        P(None, None, "shard"),
        P("shard", None),
    )
    return jax.shard_map(
        on_device,
        mesh=mesh,
        in_specs=placed,
        out_specs=(
            P(None, "shard", None),
            P(None, None, "shard"),
            P("shard", None),
            P(None, "shard", None),
            P(None, None, "shard"),
            P("shard", None),
            P(None, "shard", None),
            P(None, None, "shard"),
            P("shard", None),
            P(),
            P(),
            P(),
            P(),
        ),
        check_vma=False,
    )
```

profile of v0, /device:TPU:1, one launch (start us, length us, event | category | flops | bytes accessed | tf_op | source)
XLA Modules:
  0.0 806.5 jit_solution(3559955693259106270)
XLA Ops:
  7.2 6.5 reduce_sum.65
  13.7 66.3 %copy.25 = bf16[2,118,3072]{0,1,2:T(8,128)(2,1)} copy(bf16[2,118,3072]{2,0,1:T(2,128)(2,1)S(1)} %reduce_sum.65) | data formatting | bytes 2899968
  80.0 86.8 %reshape.30 = bf16[3072,236]{1,0:T(8,128)(2,1)} reshape(bf16[3072,118,2]{2,1,0:T(8,128)(2,1)} %bitcast.1) | data formatting | bytes 2899968
  166.9 2.2 reduce_sum.63
  169.1 6.5 reduce_sum.67
  175.9 22.9 %reduce-scatter.10.cloned.1.call-done = bf16[1536,236]{1,0:T(8,128)(2,1)} async-done(((bf16[3072,236]{1,0:T(8,128)(2,1)}), bf16[1536,236]{1,0:T(8,128)(2,1)}) %reduce-scatter.10.cloned.1.call-update) | async-done | bytes 725008
  198.8 37.8 %reshape.31 = bf16[1536,118,2]{2,1,0:T(8,128)(2,1)} reshape(bf16[1536,236]{1,0:T(8,128)(2,1)} %reduce-scatter.10.cloned.1.call-done) | data formatting | bytes 1449984
  236.6 41.9 %copy.26 = bf16[2,118,1536]{2,0,1:T(2,128)(2,1)} copy(bf16[2,118,1536]{0,1,2:T(8,128)(2,1)} %bitcast.4) | data formatting | bytes 1449984
  278.5 2.7 reduce-scatter.8.cloned.1.call-done
  281.2 373.8 %all-reduce.2 = (f32[2,1536,128]{2,1,0:T(8,128)}, f32[2,118,1536]{2,0,1:T(2,128)}, f32[512,1536]{1,0:T(8,128)S(1)}) all-reduce(bf16[2,1536,128]{2,1,0:T(8,128)(2,1)} %reduce-scatter.6.cloned.1.call-done, bf16[2,118,1536]{2,0,1:T(2,128)(2,1)} %copy.26, ...), channel_id=1, replica_groups=mesh['rep'=64,'shard'=2] {'rep'}, use_global_device_ids=true, to_apply=%region_2.0 | all-reduce | flops 1542144 | bytes 9252864 | tf_op jit(solution)/shard_map/psum | solution.py:54
  654.9 2.5 multiply_reduce_fusion.1
  657.5 2.1 multiply_reduce_fusion.2
  659.6 1.4 multiply_reduce_fusion
  662.9 4.3 psum.31
  667.9 8.4 %fusion.5 = (bf16[2,118,1536]{2,0,1:T(2,128)(2,1)}, f32[2,118,1536]{2,0,1:T(2,128)}, f32[2,118,1536]{2,0,1:T(2,128)}, f32[2,118,1536]{2,0,1:T(2,128)}) fusion(f32[2,118,1536]{2,0,1:T(2,128)} %param.16, f32[2,118,1536]{2,0,1:T(2,128)} %get-tuple-element.14, f32[]{:T(128)S(6)} %mul.157, f32[2,118,1536]{2,0,1:T(2,128)} %param.19, f32[2,118,1536]{2,0,1:T(2,128)} %param.22), kind=kLoop, calls=%fused_computation.16 | loop fusion | flops 6162432 | bytes 10874884 | tf_op jit(solution)/shard_map/convert_element_type | solution.py:68
  676.5 6.1 fusion.7
  682.6 0.3 all-gather.8.cloned.1.call-start
  682.8 7.4 fusion.3
  690.2 16.8 %all-gather.6.cloned.1.call-done = bf16[2,118,3072]{2,0,1:T(2,128)(2,1)} async-done(((bf16[2,118,1536]{2,0,1:T(2,128)(2,1)}), bf16[2,118,3072]{2,0,1:T(2,128)(2,1)}) %all-gather.6.cloned.1.call-update) | async-done | bytes 1450000 | tf_op jit(solution)/shard_map/all_gather | solution.py:68
  707.0 32.9 %all-gather.4.cloned.1.call-done = bf16[2,3072,128]{2,1,0:T(8,128)(2,1)} async-done(((bf16[2,1536,128]{2,1,0:T(8,128)(2,1)}), bf16[2,3072,128]{2,1,0:T(8,128)(2,1)}) %all-gather.4.cloned.1.call-update) | async-done | bytes 1572880 | tf_op jit(solution)/shard_map/all_gather | solution.py:67
  739.9 50.6 %all-gather.8.cloned.1.call-done = bf16[1024,1536]{1,0:T(8,128)(2,1)} async-done(((bf16[512,1536]{1,0:T(8,128)(2,1)}), bf16[1024,1536]{1,0:T(8,128)(2,1)}) %all-gather.8.cloned.1.call-update) | async-done | bytes 3145744 | tf_op jit(solution)/shard_map/all_gather | solution.py:69
  790.6 2.8 copy.36
  793.4 3.5 copy.37
  796.9 1.7 copy.38
  (18 shorter events, 0.5 us)
Async XLA Ops:
  7.2 191.6 %reduce-scatter.10.cloned.1.call-start = ((), (), s32[]{:S(2)}) async-start(), calls=%async_computation.8 | async-start | bytes 2359296
  80.0 86.8 %copy-start.1 = (bf16[2,2,3072,128]{3,2,1,0:T(8,128)(2,1)S(1)}, bf16[2,2,3072,128]{3,2,1,0:T(8,128)(2,1)}, u32[]{:S(2)}) copy-start(bf16[2,2,3072,128]{3,2,1,0:T(8,128)(2,1)} %param.12) | copy-start | bytes 9437188
  166.8 111.7 %reduce-scatter.6.cloned.1.call-start = ((), (), s32[]{:S(2)}) async-start(), calls=%async_computation.3 | async-start | bytes 2359296 | tf_op jit(solution)/shard_map/reduce_scatter | solution.py:44
  169.1 112.1 %reduce-scatter.8.cloned.1.call-start = ((), (), s32[]{:S(2)}) async-start(), calls=%async_computation.4 | async-start | bytes 4718592 | tf_op jit(solution)/shard_map/reduce_scatter | solution.py:50
  175.6 531.4 %all-gather.6.cloned.1.call-start = ((), (), s32[]{:S(2)}) async-start(), calls=%async_computation.6 | async-start | bytes 2174976 | tf_op jit(solution)/shard_map/all_gather | solution.py:68
  654.9 2.5 copy-start
  676.4 63.5 %all-gather.4.cloned.1.call-start = ((), (), s32[]{:S(2)}) async-start(), calls=%async_computation.5 | async-start | bytes 2359296 | tf_op jit(solution)/shard_map/all_gather | solution.py:67
  682.6 108.0 %all-gather.8.cloned.1.call-start = ((), (), s32[]{:S(2)}) async-start(), calls=%async_computation.7 | async-start | bytes 4718592 | tf_op jit(solution)/shard_map/all_gather | solution.py:69
  790.6 6.3 copy-start.2
Sparse Core Ops, SparseCore 0:
  166.9 31.7 reduce-scatter.9
  201.8 29.5 reduce-scatter.5
  234.3 46.8 reduce-scatter.7
  676.5 30.4 all-gather.5
  709.2 30.6 all-gather.3
  742.1 48.4 all-gather.7
where the time goes:
time: 810 us; the launch traced here: 806 us
  blocking collectives  378 us (47%)
  local copies, waits for them, and re-layouts  241 us (30%)
  waiting for transfers between devices  126 us (16%)
  other arithmetic  43.1 us (5%)
  between operations  18 us (2%)
    psum x1, blocking collectives, on_device(): blocks = lax.psum((group[0], group[1], group[2]), 'rep')  374 us
    unnamed x13, local copies, waits for them, and re-layouts  241 us
    all_gather x1, waiting for transfers between devices, on_device(): lax.all_gather(we.astype(jnp.bfloat16), 'shard', axis=0, tiled=True)  50.6 us
    all_gather x1, waiting for transfers between devices, on_device(): lax.all_gather(wx.astype(jnp.bfloat16), 'shard', axis=1, tiled=True)  32.9 us
    unnamed x7, waiting for transfers between devices  23 us
    all_gather x1, waiting for transfers between devices, on_device(): lax.all_gather(wc.astype(jnp.bfloat16), 'shard', axis=2, tiled=True)  16.8 us
  transfers between devices with their start and end apart: 6, of which 5 were waited for; matrix products, arithmetic and copies ran while one was open for 13% of the time, Pallas kernels for 0%

commit v1 on v0

--- a/solution.py
+++ b/solution.py
@@ -64,7 +64,12 @@
     wc, mc, vc = adamw_update(weight_chan, moment_chan, second_chan, mean_c, clip_factor)
     we, me, ve = adamw_update(weight_embed, moment_embed, second_embed, mean_e, clip_factor)
     gathered = (
-        lax.all_gather(wx.astype(jnp.bfloat16), "shard", axis=1, tiled=True),
+        jnp.concatenate(
+            lax.all_to_all(
+                jnp.stack([wx.astype(jnp.bfloat16)] * lax.axis_size("shard")), "shard", 0, 0
+            ),
+            axis=1,
+        ),
         lax.all_gather(wc.astype(jnp.bfloat16), "shard", axis=2, tiled=True),
         lax.all_gather(we.astype(jnp.bfloat16), "shard", axis=0, tiled=True),
     )

time: 810 us -> 789 us (0.974)
  waiting for transfers between devices: 126 us -> 74.5 us
  blocking collectives: 378 us -> 408 us
    all_gather x1 -> x0, waiting for transfers between devices: 32.9 us -> none  [on_device(): lax.all_gather(wx.astype(jnp.bfloat16), 'shard', axis=1, tiled=True)]
    all_to_all x0 -> x1, blocking collectives: none -> 29.8 us  [on_device(): lax.all_to_all(jnp.stack([wx.astype(jnp.bfloat16)] * lax.axis_size('shard...]
    all_gather x1, waiting for transfers between devices: 16.8 us -> 0.01 us  [on_device(): lax.all_gather(wc.astype(jnp.bfloat16), 'shard', axis=2, tiled=True)]
    unnamed x13 -> x12, local copies, waits for them, and re-layouts: 241 us -> 241 us
    unnamed x7 -> x6, waiting for transfers between devices: 23 us -> 23 us
  transfers between devices with their start and end apart: 6 -> 5, of which waited for: 5 -> 3; matrix products, arithmetic and copies ran while one was open for 13% -> 13% of each run, Pallas kernels for 0% -> 0%
where the time goes in v1:
time: 789 us; the launch traced here: 786 us
  blocking collectives  408 us (52%)
  local copies, waits for them, and re-layouts  243 us (31%)
  waiting for transfers between devices  74.5 us (9%)
  other arithmetic  42.5 us (5%)
  between operations  17.6 us (2%)
    psum x1, blocking collectives, on_device(): blocks = lax.psum((group[0], group[1], group[2]), 'rep')  374 us
    unnamed x12, local copies, waits for them, and re-layouts  241 us
    all_gather x1, waiting for transfers between devices, on_device(): lax.all_gather(we.astype(jnp.bfloat16), 'shard', axis=0, tiled=True)  48.9 us
    all_to_all x1, blocking collectives, on_device(): lax.all_to_all(jnp.stack([wx.astype(jnp.bfloat16)] * lax.axis_size('shard...  29.8 us
    unnamed x6, waiting for transfers between devices  23 us
  transfers between devices with their start and end apart: 5, of which 3 were waited for; matrix products, arithmetic and copies ran while one was open for 13% of the time, Pallas kernels for 0%

profile of v1, /device:TPU:1, one launch (start us, length us, event | category | flops | bytes accessed | tf_op | source)
XLA Modules:
  0.0 785.5 jit_solution(2517195768088750267)
XLA Ops:
  7.2 6.5 reduce_sum.65
  13.7 66.3 %copy.27 = bf16[2,118,3072]{0,1,2:T(8,128)(2,1)} copy(bf16[2,118,3072]{2,0,1:T(2,128)(2,1)S(1)} %reduce_sum.65) | data formatting | bytes 2899968
  80.0 86.8 %reshape.38 = bf16[3072,236]{1,0:T(8,128)(2,1)} reshape(bf16[3072,118,2]{2,1,0:T(8,128)(2,1)} %bitcast.1) | data formatting | bytes 2899968
  166.9 2.2 reduce_sum.63
  169.1 6.5 reduce_sum.67
  175.6 0.2 all-gather.3.cloned.1.call-start
  175.9 22.9 %reduce-scatter.10.cloned.1.call-done = bf16[1536,236]{1,0:T(8,128)(2,1)} async-done(((bf16[3072,236]{1,0:T(8,128)(2,1)}), bf16[1536,236]{1,0:T(8,128)(2,1)}) %reduce-scatter.10.cloned.1.call-update) | async-done | bytes 725008
  198.8 37.8 %reshape.39 = bf16[1536,118,2]{2,1,0:T(8,128)(2,1)} reshape(bf16[1536,236]{1,0:T(8,128)(2,1)} %reduce-scatter.10.cloned.1.call-done) | data formatting | bytes 1449984
  236.6 41.9 %copy.28 = bf16[2,118,1536]{2,0,1:T(2,128)(2,1)} copy(bf16[2,118,1536]{0,1,2:T(8,128)(2,1)} %bitcast.8) | data formatting | bytes 1449984
  278.5 2.7 reduce-scatter.8.cloned.1.call-done
  281.2 373.8 %all-reduce.2 = (f32[2,1536,128]{2,1,0:T(8,128)}, f32[2,118,1536]{2,0,1:T(2,128)}, f32[512,1536]{1,0:T(8,128)S(1)}) all-reduce(bf16[2,1536,128]{2,1,0:T(8,128)(2,1)} %reduce-scatter.6.cloned.1.call-done, bf16[2,118,1536]{2,0,1:T(2,128)(2,1)} %copy.28, ...), channel_id=1, replica_groups=mesh['rep'=64,'shard'=2] {'rep'}, use_global_device_ids=true, to_apply=%region_2.0 | all-reduce | flops 1542144 | bytes 9252864 | tf_op jit(solution)/shard_map/psum | solution.py:54
  654.9 2.5 multiply_reduce_fusion.1
  657.5 2.1 multiply_reduce_fusion.2
  659.6 1.4 multiply_reduce_fusion
  662.9 4.3 psum.31
  667.9 8.5 %fusion.5 = (bf16[2,118,1536]{2,0,1:T(2,128)(2,1)}, f32[2,118,1536]{2,0,1:T(2,128)}, f32[2,118,1536]{2,0,1:T(2,128)}, f32[2,118,1536]{2,0,1:T(2,128)}) fusion(f32[2,118,1536]{2,0,1:T(2,128)} %param.16, f32[2,118,1536]{2,0,1:T(2,128)} %get-tuple-element.14, f32[]{:T(128)S(6)} %mul.157, f32[2,118,1536]{2,0,1:T(2,128)} %param.19, f32[2,118,1536]{2,0,1:T(2,128)} %param.22), kind=kLoop, calls=%fused_computation.18 | loop fusion | flops 6162432 | bytes 10874884 | tf_op jit(solution)/shard_map/convert_element_type | solution.py:73
  676.5 7.3 fusion.3
  683.8 1.4 copy-done
  685.2 5.4 convert_bitcast_fusion
  690.7 29.8 %all_to_all.5 = bf16[2,2,1536,128]{3,2,1,0:T(8,128)(2,1)S(1)} all-to-all(bf16[2,2,1536,128]{3,2,1,0:T(8,128)(2,1)S(1)} %pad_maximum_fusion), channel_id=1, replica_groups=mesh['rep'=64,'shard'=2] {'shard'}, dimensions={0} | all-to-all | bytes 3145728 | tf_op jit(solution)/shard_map/all_to_all | solution.py:68
  720.5 1.2 copy.26
  721.8 48.9 %all-gather.5.cloned.1.call-done = bf16[1024,1536]{1,0:T(8,128)(2,1)} async-done(((bf16[512,1536]{1,0:T(8,128)(2,1)}), bf16[1024,1536]{1,0:T(8,128)(2,1)}) %all-gather.5.cloned.1.call-update) | async-done | bytes 3145744 | tf_op jit(solution)/shard_map/all_gather | solution.py:74
  770.6 3.5 copy.37
  774.1 3.8 copy.38
  (17 shorter events, 0.4 us)
Async XLA Ops:
  7.2 191.6 %reduce-scatter.10.cloned.1.call-start = ((), (), s32[]{:S(2)}) async-start(), calls=%async_computation.8 | async-start | bytes 2359296
  80.0 86.8 %copy-start.2 = (bf16[2,2,3072,128]{3,2,1,0:T(8,128)(2,1)S(1)}, bf16[2,2,3072,128]{3,2,1,0:T(8,128)(2,1)}, u32[]{:S(2)}) copy-start(bf16[2,2,3072,128]{3,2,1,0:T(8,128)(2,1)} %param.12) | copy-start | bytes 9437188
  166.8 111.7 %reduce-scatter.6.cloned.1.call-start = ((), (), s32[]{:S(2)}) async-start(), calls=%async_computation.4 | async-start | bytes 2359296 | tf_op jit(solution)/shard_map/reduce_scatter | solution.py:44
  169.1 112.1 %reduce-scatter.8.cloned.1.call-start = ((), (), s32[]{:S(2)}) async-start(), calls=%async_computation.5 | async-start | bytes 4718592 | tf_op jit(solution)/shard_map/reduce_scatter | solution.py:50
  175.6 546.1 %all-gather.3.cloned.1.call-start = ((), (), s32[]{:S(2)}) async-start(), calls=%async_computation.6 | async-start | bytes 2174976 | tf_op jit(solution)/shard_map/all_gather | solution.py:73
  654.9 2.5 copy-start.1
  676.4 94.2 %all-gather.5.cloned.1.call-start = ((), (), s32[]{:S(2)}) async-start(), calls=%async_computation.7 | async-start | bytes 4718592 | tf_op jit(solution)/shard_map/all_gather | solution.py:74
  683.8 1.4 copy-start
Sparse Core Ops, SparseCore 0:
  166.9 31.7 reduce-scatter.9
  201.8 29.5 reduce-scatter.5
  234.3 46.8 reduce-scatter.7
  676.5 37.8 all-gather.2
  716.6 54.0 all-gather.4
